TPU v7x, 256 devices: a whole 4x4x8 slice. The times are simulated.
256 devices in a mesh: gx: 4 (over x), gy: 8 (over z_hi, core), gz: 8 (over z_lo, y).
Axes of the slice: x: 4, y: 4, z: 8 (z_hi: 4, z_lo: 2; z = z_hi * 2 + z_lo), core: 2. Of those that a mesh axis runs over, the one named last changes fastest.
Arguments:
- fine: float32 [5, 64, 128, 1024], P(None, 'gx', 'gy', 'gz'), as said below
- shell: float32 [4, 512, 3840], P('gx', ('gy', 'gz')), as said below
- parent: int32 [4, 512], P('gx'), may hold values from 0 to 511, as said below
- link: int32 [6, 4, 8, 64], P(None, 'gx', 'gy', 'gz'), may hold values 0 or 1
Outputs:
- fine_new: float32 [5, 64, 128, 1024], P(None, 'gx', 'gy', 'gz')
- coarse_new: float32 [4, 512, 2560], P('gx', ('gy', 'gz'))
Inputs may be any that keep to these rules, and one draw needn't show every extreme that they name: Each row parent[i, :] names every slot 0 to 511 exactly once. Of the 8 blocks q = d * 8 to d * 8 + 7 of a row, at most 2 have parents among the slots o * 8 to o * 8 + 7 of any one o, and every such pair that meets at all holds exactly 2. `fine`: density and energy make pressure positive in every cell; velocities stay well below the sound speed times a few. `shell`: same physical ranges as fine.
All inputs are finite; a program needn't handle non-finite values. No bound on the sum of `link` on one device may be relied on, other than what follows from the above.
Results may differ from a plain program's by a relative error of at most 0.0003.
Values sent between devices are 32-bit elements; how exact they have to be, the bound alone decides.
No kernel may reach another device: no remote copies, remote signals or barrier semaphores. Data moves between devices by JAX's collectives and lax.ppermute only.
A program may use at most 128 MiB of HBM per device.

v0:
```python
import jax
import jax.numpy as jnp
from jax import lax
from jax.sharding import PartitionSpec as P

BS = 16
GAMMA = 1.4
LAMBDA = 0.05


def padded_2(cells, sides, width):
    for axis, dim in sides:
        count = lax.axis_size(axis)
        head = lax.slice_in_dim(cells, 0, width, axis=dim)
        tail = lax.slice_in_dim(cells, cells.shape[dim] - width, cells.shape[dim], axis=dim)
        cells = jnp.concatenate(
            [
                lax.ppermute(tail, axis, [(i, (i + 1) % count) for i in range(count)]),
                cells,
                lax.ppermute(head, axis, [((i + 1) % count, i) for i in range(count)]),
            ],
            axis=dim,
        )
    return cells


def cell_flux(state, direc):
    rho = state[0]
    mom = state[1:4]
    energy = state[4]
    vel = mom / rho[None]
    press = (GAMMA - 1.0) * (energy - 0.5 * jnp.sum(mom * vel, axis=0))
    normal = vel[direc]
    parts = [
        mom[direc],
        mom[0] * normal,
        mom[1] * normal,
        mom[2] * normal,
        (energy + press) * normal,
    ]
    parts[1 + direc] = parts[1 + direc] + press
    flux = jnp.stack(parts, axis=0)
    speed = jnp.abs(normal) + jnp.sqrt(GAMMA * press / rho)
    return (flux, speed)


def pair_face(flux_a, speed_a, value_a, flux_b, speed_b, value_b):
    return 0.5 * (flux_a + flux_b) - 0.5 * jnp.maximum(speed_a, speed_b)[None] * (value_b - value_a)


def along_axis(ext, direc):
    flux, speed = cell_flux(ext, direc)
    dim = 1 + direc
    count = ext.shape[dim]
    face = pair_face(
        lax.slice_in_dim(flux, 0, count - 1, axis=dim),
        lax.slice_in_dim(speed, 0, count - 1, axis=dim - 1),
        lax.slice_in_dim(ext, 0, count - 1, axis=dim),
        lax.slice_in_dim(flux, 1, count, axis=dim),
        lax.slice_in_dim(speed, 1, count, axis=dim - 1),
        lax.slice_in_dim(ext, 1, count, axis=dim),
    )
    return lax.slice_in_dim(face, 1, count - 1, axis=dim) - lax.slice_in_dim(
        face, 0, count - 2, axis=dim
    )


def along_blocks(state, ghost_low, ghost_high):
    nz_dev = state.shape[3]
    flux, speed = cell_flux(state, 2)
    inner = pair_face(
        jnp.roll(flux, 1, axis=3),
        jnp.roll(speed, 1, axis=2),
        jnp.roll(state, 1, axis=3),
        flux,
        speed,
        state,
    )
    low_flux, low_speed = cell_flux(ghost_low, 2)
    high_flux, high_speed = cell_flux(ghost_high, 2)
    start = pair_face(
        low_flux, low_speed, ghost_low, flux[..., 0::BS], speed[..., 0::BS], state[..., 0::BS]
    )
    finish = pair_face(
        flux[..., BS - 1 :: BS],
        speed[..., BS - 1 :: BS],
        state[..., BS - 1 :: BS],
        high_flux,
        high_speed,
        ghost_high,
    )
    plane = jnp.arange(nz_dev, dtype=jnp.int32) % BS
    left_face = jnp.where(plane == 0, jnp.repeat(start, BS, axis=3), inner)
    right_face = jnp.where(
        plane == BS - 1, jnp.repeat(finish, BS, axis=3), jnp.roll(left_face, -1, axis=3)
    )
    return right_face - left_face


def inject(coarse):
    return jnp.repeat(jnp.repeat(coarse, 2, axis=-2), 2, axis=-1)


def side_ghost(fine_face, level, links, face, nz_dev):
    coarse = inject(level[:, face]).transpose(1, 2, 0, 3).reshape(5, BS, nz_dev)
    chosen = jnp.repeat(links[:, face] == 1, BS)[None, None, :]
    return jnp.where(chosen, fine_face, coarse)


def end_ghost(fine_face, level, links, face):
    coarse = inject(level[:, face]).transpose(1, 2, 3, 0)
    chosen = (links[:, face] == 1)[None, None, None, :]
    return jnp.where(chosen, fine_face, coarse)


def restrict_state(state, nblk):
    half = BS // 2
    grouped = state.reshape(5, half, 2, half, 2, nblk, half, 2)
    means = grouped.mean(axis=(2, 4, 7))
    return means.transpose(3, 0, 1, 2, 4).reshape(nblk, -1)


def shards(fine, shell, parent, link):
    half = BS // 2
    nz_dev = fine.shape[3]
    nblk = nz_dev // BS
    row_zero = (lax.axis_index("gy") * lax.axis_size("gz") + lax.axis_index("gz")) * nblk
    parent_row = parent[0]
    mine = lax.dynamic_slice_in_dim(parent_row, row_zero, nblk)
    links = link[:, 0, 0, :].T
    width = shell.shape[2] // 2

    def selector(piece):
        count = piece.shape[1]
        onehot = (mine[:, None] == jnp.arange(count, dtype=jnp.int32)[None, :]).astype(jnp.float32)
        return jnp.dot(
            onehot, piece[0], precision=lax.Precision.HIGHEST, preferred_element_type=jnp.float32
        )

    level_now = selector(lax.all_gather(shell[:, :, :width], ("gy", "gz"), axis=1, tiled=True))
    owner_mid = 0.5 * (shell[:, :, :width] + shell[:, :, width:])
    level_mid = selector(lax.all_gather(owner_mid, ("gy", "gz"), axis=1, tiled=True))
    state = fine
    for step in range(2):
        level = (level_now if step == 0 else level_mid).reshape(nblk, 6, 5, half, half)
        padded = padded_2(state, (("gx", 1), ("gy", 2), ("gz", 3)), 1)
        ghost_x0 = side_ghost(padded[:, 0, 1:-1, 1:-1], level, links, 0, nz_dev)
        ghost_x1 = side_ghost(padded[:, -1, 1:-1, 1:-1], level, links, 1, nz_dev)
        ghost_y0 = side_ghost(padded[:, 1:-1, 0, 1:-1], level, links, 2, nz_dev)
        ghost_y1 = side_ghost(padded[:, 1:-1, -1, 1:-1], level, links, 3, nz_dev)
        ghost_z0 = end_ghost(padded[:, 1:-1, 1:-1, 0:nz_dev:BS], level, links, 4)
        ghost_z1 = end_ghost(padded[:, 1:-1, 1:-1, BS + 1 :: BS], level, links, 5)
        ext_x = jnp.concatenate([ghost_x0[:, None], state, ghost_x1[:, None]], axis=1)
        ext_y = jnp.concatenate([ghost_y0[:, :, None], state, ghost_y1[:, :, None]], axis=2)
        total = (
            along_axis(ext_x, 0) + along_axis(ext_y, 1) + along_blocks(state, ghost_z0, ghost_z1)
        )
        state = state - LAMBDA * total
    restricted = restrict_state(state, nblk)
    piece = lax.all_gather(restricted, ("gy", "gz"), axis=0, tiled=True)
    count = piece.shape[0]
    wanted = row_zero + jnp.arange(nblk, dtype=jnp.int32)
    onehot = (parent_row[None, :] == wanted[:, None]).astype(jnp.float32)
    gathered = jnp.dot(
        onehot, piece, precision=lax.Precision.HIGHEST, preferred_element_type=jnp.float32
    )
    coarse_new = gathered.reshape(1, nblk, restricted.shape[1])
    return (state, coarse_new)


def solution(mesh):
    return jax.shard_map(
        shards,
        mesh=mesh,
        in_specs=(
            P(None, "gx", "gy", "gz"),
            P("gx", ("gy", "gz"), None),
            P("gx", None),
            P(None, "gx", "gy", "gz"),
        ),
        out_specs=(P(None, "gx", "gy", "gz"), P("gx", ("gy", "gz"), None)),
        check_vma=False,
    )
```

profile of v0, /device:TPU:105, one launch (start us, length us, event | category | flops | bytes accessed | tf_op | source)
XLA Modules:
  0.0 840.2 jit_solution(8892528713839068950)
XLA Ops:
  7.2 1.5 add_multiply_fusion
  9.5 1.4 fusion.133
  11.0 2.5 collective-permute-start.1
  13.5 1.3 copy.446
  14.8 4.3 slice.630
  19.1 4.3 slice.617
  29.2 4.2 slice.628
  33.5 4.3 slice.603
  39.2 165.1 %all-gather.6.cloned.1.call-done = f32[1,512,1920]{2,1,0:T(8,128)} async-done(((f32[1,8,1920]{2,1,0:T(8,128)}), f32[1,512,1920]{2,1,0:T(8,128)}) %all-gather.6.cloned.1.call-update) | async-done | bytes 3932176 | tf_op jit(solution)/shard_map/all_gather | solution.py:142
  204.2 5.5 copy.447
  209.7 185.8 %all-gather.4.cloned.1.call-done = f32[1,512,1920]{2,1,0:T(8,128)} async-done(((f32[1,8,1920]{2,1,0:T(8,128)}), f32[1,512,1920]{2,1,0:T(8,128)}) %all-gather.4.cloned.1.call-update) | async-done | bytes 3932176 | tf_op jit(solution)/shard_map/all_gather | solution.py:140
  395.6 5.7 copy.402
  401.3 15.3 %fusion.119 = f32[8,6,5,8,8]{4,0,3,2,1:T(8,128)S(1)} fusion(f32[6,5,8,8,512]{4,3,2,1,0:T(8,128)} %bitcast.437, s32[8]{0:T(128)S(1)} %dynamic-slice_bitcast_fusion), kind=kOutput, calls=%fused_computation.287 | convolution fusion | flops 94375936 | bytes 3993632 | tf_op jit(solution)/shard_map/dot_general | solution.py:136
  416.6 13.5 %fusion.121 = f32[8,6,5,8,8]{4,0,3,2,1:T(8,128)S(1)} fusion(f32[6,5,8,8,512]{4,3,2,1,0:T(8,128)S(1)} %bitcast.438, s32[8]{0:T(128)S(1)} %dynamic-slice_bitcast_fusion), kind=kOutput, calls=%fused_computation.288 | convolution fusion | flops 94375936 | bytes 3993632 | tf_op jit(solution)/shard_map/dot_general | solution.py:136
  436.4 1.4 fusion.7
  442.3 1.2 copy.438
  444.9 1.2 copy.466
  452.1 4.4 collective-permute-done.3
  460.4 1.2 copy.429
  464.0 1.6 fusion.13
  466.2 1.9 copy.431
  468.1 1.8 copy.432
  469.9 4.2 pad_maximum_fusion
  474.1 7.1 slice.619
  481.2 7.1 slice.607
  488.3 1.2 bitcast_select_fusion.2
  492.5 3.1 broadcast_in_dim.226
  495.6 4.7 reshape.314
  500.2 1.6 multiply_subtract_fusion.2
  501.8 3.1 broadcast_in_dim.231
  504.9 4.7 reshape.317
  509.6 2.0 fusion.26
  512.9 1.3 collective-permute-start.6
  516.5 4.3 slice.708
  520.8 4.4 slice.696
  528.4 4.2 slice.706
  532.6 4.4 slice.683
  537.0 1.7 collective-permute-start.7
  538.8 1.9 collective-permute-done.7
  541.0 2.3 collective-permute-start.8
  543.7 1.4 fusion.5
  545.1 3.9 collective-permute-done.9
  552.2 1.3 copy.458
  554.1 2.4 collective-permute-start.11
  556.5 1.6 fusion.11
  558.2 1.6 collective-permute-done.10
  560.6 1.8 copy.461
  562.4 3.9 pad_maximum_fusion.1
  566.3 6.2 slice.697
  572.5 7.1 slice.686
  579.6 1.7 bitcast_select_fusion
  584.0 3.1 broadcast_in_dim.242
  587.1 4.7 reshape.332
  591.7 1.5 multiply_subtract_fusion
  593.2 3.1 broadcast_in_dim.245
  596.3 4.7 reshape.335
  601.0 1.6 fusion.31
  603.4 8.7 %copy.470 = f32[5,16,16,128]{0,3,2,1:T(8,128)} copy(f32[5,16,16,128]{3,1,2,0:T(8,128)S(1)} %fusion.19) | data formatting | bytes 1310720 | tf_op jit(solution)/shard_map/sub | solution.py:158
  612.0 13.3 %reduce_sum.109 = f32[5,8,8,8,8]{0,4,3,2,1:T(8,128)} reduce(f32[5,8,2,8,2,8,8,2]{0,7,6,5,4,3,2,1:T(2,128)} %bitcast.434, f32[]{:T(128)} %constant.33.clone.1), dimensions={2,4,7}, to_apply=%region_10.11 | reduce | flops 143360 | bytes 737284 | tf_op jit(solution)/shard_map/reduce_sum | solution.py:119
  625.3 1.8 multiply_bitcast_fusion
  627.1 4.8 copy.471
  631.8 2.6 reshape.337
  635.5 192.8 %all-gather.8.cloned.1.call-done = f32[512,2560]{1,0:T(8,128)} async-done(((f32[8,2560]{1,0:T(8,128)}), f32[512,2560]{1,0:T(8,128)}) %all-gather.8.cloned.1.call-update) | async-done | bytes 5242896 | tf_op jit(solution)/shard_map/all_gather | solution.py:160
  828.3 4.9 convolution_bitcast_fusion
  (331 shorter events, 51.6 us)
Async XLA Ops:
  7.2 197.1 %all-gather.6.cloned.1.call-start = ((), (), s32[]{:S(2)}) async-start(), calls=%async_computation.1 | async-start | bytes 3993600 | tf_op jit(solution)/shard_map/all_gather | solution.py:142
  8.7 386.8 %all-gather.4.cloned.1.call-start = ((), (), s32[]{:S(2)}) async-start(), calls=%async_computation | async-start | bytes 3993600 | tf_op jit(solution)/shard_map/all_gather | solution.py:140
  9.5 818.8 %all-gather.8.cloned.1.call-start = ((), (), s32[]{:S(2)}) async-start(), calls=%async_computation.2 | async-start | bytes 5324800 | tf_op jit(solution)/shard_map/all_gather | solution.py:160
  11.0 420.6 %collective-permute-start.1 = (f32[5,1,16,128]{3,1,2,0:T(1,128)}, f32[5,1,16,128]{3,1,2,0:T(1,128)S(1)}, u32[]{:S(2)}, u32[]{:S(2)}) collective-permute-start(f32[5,1,16,128]{3,1,2,0:T(1,128)} %bitcast.15), channel_id=1, source_target_pairs={{64,0},{128,64},{192,128},{0,192},{65,1},{129,65},{193,129},{1,193... | collective-permute-start | bytes 122888 | tf_op jit(solution)/shard_map/ppermute | solution.py:20
  13.5 420.2 %collective-permute-start = (f32[5,1,16,128]{3,1,2,0:T(1,128)}, f32[5,1,16,128]{3,1,2,0:T(1,128)S(1)}, u32[]{:S(2)}, u32[]{:S(2)}) collective-permute-start(f32[5,1,16,128]{3,1,2,0:T(1,128)} %bitcast.2), channel_id=1, source_target_pairs={{0,64},{64,128},{128,192},{192,0},{1,65},{65,129},{129,193},{193,1... | collective-permute-start | bytes 122888 | tf_op jit(solution)/shard_map/ppermute | solution.py:18
  28.1 9.7 %copy-start.56 = (s32[6,1,1,8]{3,2,1,0:T(1,128)S(1)}, s32[6,1,1,8]{3,2,1,0:T(1,128)}, u32[]{:S(2)}) copy-start(s32[6,1,1,8]{3,2,1,0:T(1,128)} %param.7) | copy-start | bytes 580
  28.1 11.0 %copy-start.57 = (s32[1,512]{1,0:T(1,128)S(1)}, s32[1,512]{1,0:T(1,128)}, u32[]{:S(2)}) copy-start(s32[1,512]{1,0:T(1,128)} %param.6) | copy-start | bytes 6148
  401.3 15.3 %copy-start = (f32[1920,512]{1,0:T(8,128)S(1)}, f32[1920,512]{1,0:T(8,128)}, u32[]{:S(2)}) copy-start(f32[1920,512]{1,0:T(8,128)} %copy.402) | copy-start | bytes 11796484
  431.6 27.5 %copy-start.22 = (f32[5,1,16,128]{3,1,2,0:T(1,128)}, f32[5,1,16,128]{3,1,2,0:T(1,128)S(1)}, u32[]{:S(2)}) copy-start(f32[5,1,16,128]{3,1,2,0:T(1,128)S(1)} %collective-permute-done.1) | copy-start | bytes 122884
  433.7 25.4 %copy-start.24 = (f32[5,1,16,128]{3,1,2,0:T(1,128)}, f32[5,1,16,128]{3,1,2,0:T(1,128)S(1)}, u32[]{:S(2)}) copy-start(f32[5,1,16,128]{3,1,2,0:T(1,128)S(1)} %collective-permute-done) | copy-start | bytes 122884
  435.5 15.8 %collective-permute-start.2 = (f32[5,18,1,128]{3,1,2,0:T(8,128)}, f32[5,18,1,128]{3,1,2,0:T(8,128)}, u32[]{:S(2)}, u32[]{:S(2)}) collective-permute-start(f32[5,18,1,128]{3,1,2,0:T(8,128)} %get-tuple-element.58), channel_id=1, source_target_pairs={{0,8},{8,16},{16,24},{24,32},{32,40},{40,48},{48,56},{56,0},{1,9},... | collective-permute-start | bytes 138248 | tf_op jit(solution)/shard_map/ppermute | solution.py:18
  436.4 2.2 copy-start.30
  444.1 1.9 copy-start.31
  448.4 2.3 copy-start.55
  450.7 5.8 collective-permute-start.3
  452.1 4.4 copy-start.48
  456.5 2.6 copy-start.44
  462.3 7.6 copy-start.23
  462.3 7.6 copy-start.25
  462.3 7.6 copy-start.45
  462.3 5.8 collective-permute-start.5
  463.0 3.3 collective-permute-start.4
  474.1 14.2 %copy-start.7 = (f32[8,5,16,16]{0,2,3,1:T(8,128)S(1)}, f32[8,5,16,16]{0,2,3,1:T(8,128)}, u32[]{:S(2)}) copy-start(f32[8,5,16,16]{0,2,3,1:T(8,128)} %copy.438) | copy-start | bytes 122884
  488.3 1.4 copy-start.34
  489.6 1.3 copy-start.6
  489.6 1.3 copy-start.8
  491.0 1.3 copy-start.11
  495.6 4.7 copy-start.9
  504.9 4.7 copy-start.1
  504.9 4.7 copy-start.15
  504.9 4.7 copy-start.37
  509.6 2.3 copy-start.2
  509.6 2.3 copy-start.19
  509.6 2.3 copy-start.58
  512.9 25.8 %collective-permute-start.6 = (f32[5,1,16,128]{3,1,2,0:T(1,128)S(1)}, f32[5,1,16,128]{3,1,2,0:T(1,128)S(1)}, u32[]{:S(2)}, u32[]{:S(2)}) collective-permute-start(f32[5,1,16,128]{3,1,2,0:T(1,128)S(1)} %get-tuple-element.72), channel_id=1, source_target_pairs={{0,64},{64,128},{128,192},{192,0},{1,65},{65,129},{129,193},{193,1... | collective-permute-start | bytes 122888 | tf_op jit(solution)/shard_map/ppermute | solution.py:18
  525.2 13.5 %copy-start.54 = (f32[5,1,16,128]{3,1,2,0:T(1,128)S(1)}, f32[5,1,16,128]{3,1,2,0:T(1,128)}, u32[]{:S(2)}) copy-start(f32[5,1,16,128]{3,1,2,0:T(1,128)} %reshape.320) | copy-start | bytes 122884
  526.3 14.4 %copy-start.53 = (f32[5,1,16,128]{3,1,2,0:T(1,128)S(1)}, f32[5,1,16,128]{3,1,2,0:T(1,128)}, u32[]{:S(2)}) copy-start(f32[5,1,16,128]{3,1,2,0:T(1,128)} %reshape.323) | copy-start | bytes 122884
  537.0 3.6 collective-permute-start.7
  538.7 12.9 %copy-start.26 = (f32[5,1,16,128]{3,1,2,0:T(1,128)}, f32[5,1,16,128]{3,1,2,0:T(1,128)S(1)}, u32[]{:S(2)}) copy-start(f32[5,1,16,128]{3,1,2,0:T(1,128)S(1)} %collective-permute-done.6) | copy-start | bytes 122884
  540.7 11.0 %copy-start.28 = (f32[5,1,16,128]{3,1,2,0:T(1,128)}, f32[5,1,16,128]{3,1,2,0:T(1,128)S(1)}, u32[]{:S(2)}) copy-start(f32[5,1,16,128]{3,1,2,0:T(1,128)S(1)} %collective-permute-done.7) | copy-start | bytes 122884
  541.0 4.1 collective-permute-start.8
  543.3 5.8 collective-permute-start.9
  543.7 1.4 copy-start.52
  543.7 5.4 copy-start.51
  545.1 6.6 copy-start.40
  545.1 3.9 copy-start.47
  549.1 2.6 copy-start.42
  554.1 8.3 copy-start.27
  554.1 8.3 copy-start.29
  554.1 8.3 copy-start.41
  554.1 8.3 copy-start.43
  554.1 6.5 collective-permute-start.11
  556.5 3.2 collective-permute-start.10
  579.6 1.9 copy-start.36
  582.3 1.3 copy-start.13
  582.3 1.5 copy-start.14
  587.1 4.7 copy-start.12
  587.1 4.7 copy-start.39
  596.3 4.7 copy-start.16
  596.3 4.7 copy-start.17
  596.3 4.7 copy-start.38
  601.0 1.9 copy-start.3
  601.0 1.9 copy-start.18
  601.0 1.9 copy-start.59
  (11 other events, 9.8 us)
Sparse Core Ops, SparseCore 0:
  10.4 193.8 all-gather.5
  206.1 189.4 all-gather.3
  634.6 193.6 all-gather.7
where the time goes:
time: 846 us; the launch traced here: 840 us
  waiting for transfers between devices  557 us (66%)
  local copies, waits for them, and re-layouts  169 us (20%)
  other arithmetic  52.7 us (6%)
  matrix products  33.7 us (4%)
  between operations  15.5 us (2%)
  starting transfers between devices  12.5 us (1%)
    all_gather x1, waiting for transfers between devices, shards(): piece = lax.all_gather(restricted, ('gy', 'gz'), axis=0, tiled=True)  193 us
    all_gather x1, waiting for transfers between devices, shards(): lax.all_gather(shell[:, :, :width], ('gy', 'gz'), axis=1, tiled=True)  186 us
    all_gather x1, waiting for transfers between devices, shards(): lax.all_gather(owner_mid, ('gy', 'gz'), axis=1, tiled=True)  165 us
    dot_general x2, matrix products, selector(): jnp.dot(onehot, piece[0], precision=lax.Precision.HIGHEST, preferred_elem...  28.8 us
  transfers between devices with their start and end apart: 15, of which 8 were waited for; matrix products, arithmetic and copies ran while one was open for 14% of the time, Pallas kernels for 0%

commit v1 on v0

--- a/solution.py
+++ b/solution.py
@@ -137,7 +137,14 @@
             onehot, piece[0], precision=lax.Precision.HIGHEST, preferred_element_type=jnp.float32
         )
 
-    level_now = selector(lax.all_gather(shell[:, :, :width], ("gy", "gz"), axis=1, tiled=True))
+    level_now = selector(
+        jnp.concatenate(
+            lax.all_to_all(
+                jnp.stack([shell[:, :, :width]] * lax.axis_size(("gy", "gz"))), ("gy", "gz"), 0, 0
+            ),
+            axis=1,
+        )
+    )
     owner_mid = 0.5 * (shell[:, :, :width] + shell[:, :, width:])
     level_mid = selector(lax.all_gather(owner_mid, ("gy", "gz"), axis=1, tiled=True))
     state = fine

time: 846 us -> 692 us (0.82)
  waiting for transfers between devices: 557 us -> 384 us
  starting transfers between devices: 12.5 us -> 23.8 us
    all_gather x1 -> x0, waiting for transfers between devices: 186 us -> none  [shards(): lax.all_gather(shell[:, :, :width], ('gy', 'gz'), axis=1, tiled=True)]
    all_gather x1, waiting for transfers between devices: 165 us -> 179 us  [shards(): lax.all_gather(owner_mid, ('gy', 'gz'), axis=1, tiled=True)]
    all_to_all x0 -> x1, starting transfers between devices: none -> 11.4 us  [shards(): lax.all_to_all(jnp.stack([shell[:, :, :width]] * lax.axis_size(('gy', 'gz...]
  transfers between devices with their start and end apart: 15 -> 15, of which waited for: 8 -> 7; matrix products, arithmetic and copies ran while one was open for 14% -> 18% of each run, Pallas kernels for 0% -> 0%
where the time goes in v1:
time: 692 us; the launch traced here: 685 us
  waiting for transfers between devices  384 us (55%)
  local copies, waits for them, and re-layouts  175 us (25%)
  other arithmetic  52.6 us (8%)
  matrix products  34.7 us (5%)
  starting transfers between devices  23.8 us (3%)
  between operations  15.8 us (2%)
    all_gather x1, waiting for transfers between devices, shards(): piece = lax.all_gather(restricted, ('gy', 'gz'), axis=0, tiled=True)  193 us
    all_gather x1, waiting for transfers between devices, shards(): lax.all_gather(owner_mid, ('gy', 'gz'), axis=1, tiled=True)  179 us
    dot_general x2, matrix products, selector(): jnp.dot(onehot, piece[0], precision=lax.Precision.HIGHEST, preferred_elem...  29.9 us
    slice x2, local copies, waits for them, and re-layouts, shards(): ghost_z1 = end_ghost(padded[:, 1:-1, 1:-1, BS + 1::BS], level, links, 5)  14.2 us
  transfers between devices with their start and end apart: 15, of which 7 were waited for; matrix products, arithmetic and copies ran while one was open for 18% of the time, Pallas kernels for 0%

profile of v1, /device:TPU:105, one launch (start us, length us, event | category | flops | bytes accessed | tf_op | source)
XLA Modules:
  0.0 685.5 jit_solution(4618734804135309588)
XLA Ops:
  7.2 1.5 add_multiply_fusion
  8.7 2.2 stack.22
  10.9 11.4 %all-to-all-start = ((f32[64,1,8,1920]{3,2,1,0:T(8,128)}), f32[64,1,8,1920]{3,2,1,0:T(8,128)}, u32[]{:S(2)}, u32[]{:S(2)}) async-start(f32[64,1,8,1920]{3,2,1,0:T(8,128)} %stack.22), calls=%async_computation | async-start | bytes 7864320 | tf_op jit(solution)/shard_map/all_to_all | solution.py:142
  23.0 2.5 collective-permute-start.1
  25.7 4.3 slice.633
  30.0 4.4 slice.620
  39.6 4.3 slice.631
  43.9 4.4 slice.606
  50.6 179.5 %all-gather.3.cloned.1.call-done = f32[1,512,1920]{2,1,0:T(8,128)} async-done(((f32[1,8,1920]{2,1,0:T(8,128)}), f32[1,512,1920]{2,1,0:T(8,128)}) %all-gather.3.cloned.1.call-update) | async-done | bytes 3932176 | tf_op jit(solution)/shard_map/all_gather | solution.py:149
  230.0 5.4 copy.447
  235.5 5.8 copy.402
  241.3 16.3 %fusion.119 = f32[8,6,5,8,8]{4,0,3,2,1:T(8,128)} fusion(f32[6,5,8,8,512]{4,3,2,1,0:T(8,128)} %bitcast.439, s32[8]{0:T(128)S(1)} %dynamic-slice_bitcast_fusion), kind=kOutput, calls=%fused_computation.288 | convolution fusion | flops 94375936 | bytes 3993632 | tf_op jit(solution)/shard_map/dot_general | solution.py:136
  257.6 13.5 %fusion.121 = f32[8,6,5,8,8]{4,0,3,2,1:T(8,128)S(1)} fusion(f32[6,5,8,8,512]{4,3,2,1,0:T(8,128)S(1)} %bitcast.440, s32[8]{0:T(128)S(1)} %dynamic-slice_bitcast_fusion), kind=kOutput, calls=%fused_computation.289 | convolution fusion | flops 94375936 | bytes 3993632 | tf_op jit(solution)/shard_map/dot_general | solution.py:136
  276.6 1.4 fusion.7
  295.2 4.4 collective-permute-done.3
  302.5 1.7 fusion.129
  304.2 1.9 copy.429
  306.1 1.9 copy.430
  308.0 1.6 collective-permute-start.4
  309.6 1.5 fusion.13
  311.2 1.8 copy.431
  313.0 1.8 copy.432
  314.9 4.3 pad_maximum_fusion
  319.1 7.0 %slice.622 = f32[5,16,16,8]{3,1,2,0:T(8,128)} slice(f32[5,18,18,130]{3,1,2,0:T(8,128)} %pad_maximum_fusion), slice={[0:5:1], [1:17:1], [1:17:1], [0:128:16]} | slice | bytes 81920 | tf_op jit(solution)/shard_map/slice | solution.py:158
  326.1 7.1 %slice.610 = f32[5,16,16,8]{3,1,2,0:T(8,128)} slice(f32[5,18,18,130]{3,1,2,0:T(8,128)} %pad_maximum_fusion), slice={[0:5:1], [1:17:1], [1:17:1], [17:130:16]} | slice | bytes 81920 | tf_op jit(solution)/shard_map/slice | solution.py:159
  333.2 1.4 bitcast_select_fusion.2
  338.0 3.1 broadcast_in_dim.226
  341.1 4.7 reshape.317
  345.7 1.7 multiply_subtract_fusion.2
  347.4 3.1 broadcast_in_dim.231
  350.5 4.7 reshape.320
  355.2 1.9 fusion.26
  358.4 1.3 collective-permute-start.6
  362.1 4.3 slice.711
  366.4 4.3 slice.699
  373.9 4.3 slice.709
  378.2 4.4 slice.686
  382.6 1.7 collective-permute-start.7
  384.3 1.3 collective-permute-done.7
  386.0 2.6 collective-permute-start.8
  389.0 1.4 fusion.5
  390.4 3.9 collective-permute-done.9
  397.5 1.2 copy.458
  399.4 2.0 collective-permute-start.11
  401.4 1.5 fusion.11
  403.0 1.7 collective-permute-done.10
  405.5 1.8 copy.461
  407.4 3.9 pad_maximum_fusion.1
  411.3 6.2 slice.700
  417.5 7.1 %slice.689 = f32[5,16,16,8]{3,1,2,0:T(8,128)} slice(f32[5,18,18,130]{3,1,2,0:T(8,128)} %pad_maximum_fusion.1), slice={[0:5:1], [1:17:1], [1:17:1], [17:130:16]} | slice | bytes 81920 | tf_op jit(solution)/shard_map/slice | solution.py:159
  424.5 1.7 bitcast_select_fusion
  429.0 3.1 broadcast_in_dim.242
  432.0 4.7 reshape.335
  436.7 1.5 multiply_subtract_fusion
  438.2 3.1 broadcast_in_dim.245
  441.2 4.7 reshape.338
  446.0 1.6 fusion.31
  448.3 8.8 %copy.470 = f32[5,16,16,128]{0,3,2,1:T(8,128)} copy(f32[5,16,16,128]{3,1,2,0:T(8,128)S(1)} %fusion.19) | data formatting | bytes 1310720 | tf_op jit(solution)/shard_map/sub | solution.py:165
  457.1 13.3 %reduce_sum.109 = f32[5,8,8,8,8]{0,4,3,2,1:T(8,128)} reduce(f32[5,8,2,8,2,8,8,2]{0,7,6,5,4,3,2,1:T(2,128)} %bitcast.436, f32[]{:T(128)} %constant.33.clone.1), dimensions={2,4,7}, to_apply=%region_10.11 | reduce | flops 143360 | bytes 737284 | tf_op jit(solution)/shard_map/reduce_sum | solution.py:119
  470.3 1.8 multiply_bitcast_fusion
  472.1 4.8 copy.471
  476.9 2.6 reshape.340
  480.6 192.8 %all-gather.5.cloned.1.call-done = f32[512,2560]{1,0:T(8,128)} async-done(((f32[8,2560]{1,0:T(8,128)}), f32[512,2560]{1,0:T(8,128)}) %all-gather.5.cloned.1.call-update) | async-done | bytes 5242896 | tf_op jit(solution)/shard_map/all_gather | solution.py:167
  673.3 4.9 convolution_bitcast_fusion
  (315 shorter events, 53.4 us)
Async XLA Ops:
  7.2 222.9 %all-gather.3.cloned.1.call-start = ((), (), s32[]{:S(2)}) async-start(), calls=%async_computation.1 | async-start | bytes 3993600 | tf_op jit(solution)/shard_map/all_gather | solution.py:149
  10.9 11.5 %copy-start.1 = (f32[5,16,16,128]{3,2,1,0:T(8,128)S(1)}, f32[5,16,16,128]{3,2,1,0:T(8,128)}, u32[]{:S(2)}) copy-start(f32[5,16,16,128]{3,2,1,0:T(8,128)} %param.4) | copy-start | bytes 1966084
  10.9 224.6 %all-to-all-start = ((f32[64,1,8,1920]{3,2,1,0:T(8,128)}), f32[64,1,8,1920]{3,2,1,0:T(8,128)}, u32[]{:S(2)}, u32[]{:S(2)}) async-start(f32[64,1,8,1920]{3,2,1,0:T(8,128)} %stack.22), calls=%async_computation | async-start | bytes 7864320 | tf_op jit(solution)/shard_map/all_to_all | solution.py:142
  22.3 651.0 %all-gather.5.cloned.1.call-start = ((), (), s32[]{:S(2)}) async-start(), calls=%async_computation.2 | async-start | bytes 5324800 | tf_op jit(solution)/shard_map/all_gather | solution.py:167
  23.0 249.5 %collective-permute-start.1 = (f32[5,1,16,128]{3,1,2,0:T(1,128)S(1)}, f32[5,1,16,128]{3,1,2,0:T(1,128)S(1)}, u32[]{:S(2)}, u32[]{:S(2)}) collective-permute-start(f32[5,1,16,128]{3,1,2,0:T(1,128)S(1)} %bitcast.470), channel_id=1, source_target_pairs={{64,0},{128,64},{192,128},{0,192},{65,1},{129,65},{193,129},{1,193... | collective-permute-start | bytes 122888 | tf_op jit(solution)/shard_map/ppermute | solution.py:20
  25.4 249.2 %collective-permute-start = (f32[5,1,16,128]{3,1,2,0:T(1,128)}, f32[5,1,16,128]{3,1,2,0:T(1,128)S(1)}, u32[]{:S(2)}, u32[]{:S(2)}) collective-permute-start(f32[5,1,16,128]{3,1,2,0:T(1,128)} %bitcast.2), channel_id=1, source_target_pairs={{0,64},{64,128},{128,192},{192,0},{1,65},{65,129},{129,193},{193,1... | collective-permute-start | bytes 122888 | tf_op jit(solution)/shard_map/ppermute | solution.py:18
  38.5 9.8 %copy-start.47 = (s32[6,1,1,8]{3,2,1,0:T(1,128)S(1)}, s32[6,1,1,8]{3,2,1,0:T(1,128)}, u32[]{:S(2)}) copy-start(s32[6,1,1,8]{3,2,1,0:T(1,128)} %param.7) | copy-start | bytes 580
  38.5 12.0 %copy-start.48 = (s32[1,512]{1,0:T(1,128)S(1)}, s32[1,512]{1,0:T(1,128)}, u32[]{:S(2)}) copy-start(s32[1,512]{1,0:T(1,128)} %param.6) | copy-start | bytes 6148
  241.3 16.4 %copy-start = (f32[1920,512]{1,0:T(8,128)S(1)}, f32[1920,512]{1,0:T(8,128)}, u32[]{:S(2)}) copy-start(f32[1920,512]{1,0:T(8,128)} %copy.402) | copy-start | bytes 11796484
  276.2 18.2 %collective-permute-start.2 = (f32[5,18,1,128]{3,1,2,0:T(8,128)}, f32[5,18,1,128]{3,1,2,0:T(8,128)}, u32[]{:S(2)}, u32[]{:S(2)}) collective-permute-start(f32[5,18,1,128]{3,1,2,0:T(8,128)} %get-tuple-element.58), channel_id=1, source_target_pairs={{0,8},{8,16},{16,24},{24,32},{32,40},{40,48},{48,56},{56,0},{1,9},... | collective-permute-start | bytes 138248 | tf_op jit(solution)/shard_map/ppermute | solution.py:18
  276.6 1.4 copy-start.4
  292.7 1.1 copy-start.46
  293.8 5.9 collective-permute-start.3
  295.2 4.5 copy-start.37
  300.6 0.9 copy-start.5
  304.2 5.4 copy-start.38
  304.2 5.4 copy-start.41
  308.0 5.1 collective-permute-start.5
  308.0 3.2 collective-permute-start.4
  333.2 1.6 copy-start.25
  334.6 1.8 copy-start.7
  334.6 1.8 copy-start.8
  336.5 1.1 copy-start.9
  336.5 1.3 copy-start.10
  341.1 4.7 copy-start.30
  350.5 4.7 copy-start.14
  350.5 4.7 copy-start.28
  355.1 2.2 copy-start.2
  355.2 2.2 copy-start.18
  355.2 2.2 copy-start.51
  358.4 25.8 %collective-permute-start.6 = (f32[5,1,16,128]{3,1,2,0:T(1,128)S(1)}, f32[5,1,16,128]{3,1,2,0:T(1,128)S(1)}, u32[]{:S(2)}, u32[]{:S(2)}) collective-permute-start(f32[5,1,16,128]{3,1,2,0:T(1,128)S(1)} %get-tuple-element.72), channel_id=1, source_target_pairs={{0,64},{64,128},{128,192},{192,0},{1,65},{65,129},{129,193},{193,1... | collective-permute-start | bytes 122888 | tf_op jit(solution)/shard_map/ppermute | solution.py:18
  370.7 13.5 %copy-start.45 = (f32[5,1,16,128]{3,1,2,0:T(1,128)S(1)}, f32[5,1,16,128]{3,1,2,0:T(1,128)}, u32[]{:S(2)}) copy-start(f32[5,1,16,128]{3,1,2,0:T(1,128)} %reshape.323) | copy-start | bytes 122884
  370.7 13.5 %copy-start.50 = (pred[128]{0:T(512)(128)(4,1)S(1)}, pred[128]{0:T(512)(128)(4,1)}, u32[]{:S(2)}) copy-start(pred[128]{0:T(512)(128)(4,1)} %broadcast_in_dim.203) | copy-start | bytes 388
  371.8 13.9 %copy-start.44 = (f32[5,1,16,128]{3,1,2,0:T(1,128)S(1)}, f32[5,1,16,128]{3,1,2,0:T(1,128)}, u32[]{:S(2)}) copy-start(f32[5,1,16,128]{3,1,2,0:T(1,128)} %reshape.326) | copy-start | bytes 122884
  371.8 13.9 %copy-start.49 = (pred[128]{0:T(512)(128)(4,1)S(1)}, pred[128]{0:T(512)(128)(4,1)}, u32[]{:S(2)}) copy-start(pred[128]{0:T(512)(128)(4,1)} %broadcast_in_dim.208) | copy-start | bytes 388
  382.6 3.0 collective-permute-start.7
  384.3 12.7 %copy-start.21 = (f32[5,1,16,128]{3,1,2,0:T(1,128)}, f32[5,1,16,128]{3,1,2,0:T(1,128)S(1)}, u32[]{:S(2)}) copy-start(f32[5,1,16,128]{3,1,2,0:T(1,128)S(1)} %collective-permute-done.6) | copy-start | bytes 122884
  385.6 11.3 %copy-start.23 = (f32[5,1,16,128]{3,1,2,0:T(1,128)}, f32[5,1,16,128]{3,1,2,0:T(1,128)S(1)}, u32[]{:S(2)}) copy-start(f32[5,1,16,128]{3,1,2,0:T(1,128)S(1)} %collective-permute-done.7) | copy-start | bytes 122884
  386.0 4.4 collective-permute-start.8
  388.6 5.8 collective-permute-start.9
  389.0 1.4 copy-start.43
  389.0 5.4 copy-start.42
  390.4 6.6 copy-start.32
  390.4 3.9 copy-start.36
  394.3 2.6 copy-start.34
  395.4 0.9 copy-start.6
  399.4 8.0 %copy-start.22 = (f32[5,1,16,128]{3,1,2,0:T(1,128)S(1)}, f32[5,1,16,128]{3,1,2,0:T(1,128)}, u32[]{:S(2)}) copy-start(f32[5,1,16,128]{3,1,2,0:T(1,128)} %copy-done.21) | copy-start | bytes 122884
  399.4 8.0 %copy-start.24 = (f32[5,1,16,128]{3,1,2,0:T(1,128)S(1)}, f32[5,1,16,128]{3,1,2,0:T(1,128)}, u32[]{:S(2)}) copy-start(f32[5,1,16,128]{3,1,2,0:T(1,128)} %copy-done.23) | copy-start | bytes 122884
  399.4 8.0 %copy-start.33 = (f32[5,18,1,128]{3,1,2,0:T(8,128)S(1)}, f32[5,18,1,128]{3,1,2,0:T(8,128)}, u32[]{:S(2)}) copy-start(f32[5,18,1,128]{3,1,2,0:T(8,128)} %copy-done.32) | copy-start | bytes 138244
  399.4 8.0 %copy-start.35 = (f32[5,18,1,128]{3,1,2,0:T(8,128)S(1)}, f32[5,18,1,128]{3,1,2,0:T(8,128)}, u32[]{:S(2)}) copy-start(f32[5,18,1,128]{3,1,2,0:T(8,128)} %copy-done.34) | copy-start | bytes 138244
  399.4 6.1 collective-permute-start.11
  401.4 3.3 collective-permute-start.10
  424.5 1.9 copy-start.27
  426.4 1.0 copy-start.26
  427.2 0.9 copy-start.20
  427.2 1.3 copy-start.12
  427.2 1.5 copy-start.13
  432.0 4.7 copy-start.11
  432.0 4.7 copy-start.31
  441.2 4.7 copy-start.15
  441.2 4.7 copy-start.16
  441.2 4.7 copy-start.29
  446.0 1.9 copy-start.3
  446.0 1.9 copy-start.17
  (3 other events, 2.1 us)
Sparse Core Ops, SparseCore 0:
  10.4 219.6 all-gather.2
  479.6 193.6 all-gather.4
